TPU v7x, 512 devices: a whole 4x8x8 slice. The times are simulated.
512 devices in a mesh: blk: 64 (over x, z, y_hi), dp: 8 (over y_lo, core).
Axes of the slice: x: 4, y: 8 (y_hi: 2, y_lo: 4; y = y_hi * 4 + y_lo), z: 8, core: 2. Of those that a mesh axis runs over, the one named last changes fastest.
Arguments:
- input_field: bfloat16 [262144, 2048], P('blk', 'dp'), may hold values from -6 to 6
- target_field: bfloat16 [262144, 2048], P('blk', 'dp'), may hold values from -6 to 6
- first_factor: bfloat16 [256, 1024, 256], P('dp', 'blk'), may hold values from -0.375 to 0.375
- second_factor: bfloat16 [256, 1024, 256], P('dp', 'blk'), may hold values from -0.375 to 0.375
Outputs:
- first_grad: bfloat16 [256, 1024, 256], P('dp', 'blk')
- second_grad: bfloat16 [256, 1024, 256], P('dp', 'blk')
All inputs are finite; a program needn't handle non-finite values.
Results may differ from a plain program's by a relative error of at most 0.012.
Values may be sent and summed in bfloat16 or wider, within the bound.
No kernel may reach another device: no remote copies, remote signals or barrier semaphores. Data moves between devices by JAX's collectives and lax.ppermute only.
A program may use at most 64 MiB of HBM per device.

v0:
```python
import math
import jax
import jax.numpy as jnp
from jax import lax
from jax.sharding import PartitionSpec as P

NB = 1024
BS = 256
tanh_scale = 0.7978845608028654
cubic_coef = 0.044715


def gelu_value(values):
    inner = jnp.tanh(tanh_scale * (values + cubic_coef * values * values * values))
    return 0.5 * values * (1.0 + inner)


def gelu_slope(values):
    inner = jnp.tanh(tanh_scale * (values + cubic_coef * values * values * values))
    return 0.5 * (1.0 + inner) + 0.5 * values * (1.0 - inner * inner) * tanh_scale * (
        1.0 + 3.0 * cubic_coef * values * values
    )


def shards(input_field, target_field, first_factor, second_factor):
    block_count = first_factor.shape[1]
    block_size = first_factor.shape[2]
    second_rows_local = second_factor.shape[0]
    row_count = input_field.shape[1]
    replica_count = lax.axis_size("dp")
    group_count = NB // BS
    inner_count = block_count // group_count
    scale_factor = 1.0 / math.sqrt(row_count * replica_count)
    inputs = input_field.reshape(block_count, block_size, row_count)
    first_full = lax.all_gather(first_factor, "dp", axis=0, tiled=True)
    pre_act = jnp.einsum("bkr,kbi->bir", inputs, first_full, preferred_element_type=jnp.float32)
    activated = gelu_value(pre_act).astype(jnp.bfloat16)
    received = lax.all_to_all(activated, "blk", split_axis=1, concat_axis=0, tiled=True)
    permuted = received.reshape(group_count, block_size, inner_count, row_count)
    targets = target_field.reshape(inner_count, group_count, block_size, row_count)
    piece_rows = lax.all_gather(second_factor, "dp", axis=0, tiled=True)
    count = piece_rows.shape[0]
    permuted_part = permuted
    split_part = piece_rows.reshape(count, inner_count, group_count, block_size)
    predicted = jnp.einsum(
        "gcir,cigj->igjr", permuted_part, split_part, preferred_element_type=jnp.float32
    )
    residual = ((predicted - targets.astype(jnp.float32)) * scale_factor).astype(jnp.bfloat16)
    piece_rows = lax.all_gather(second_factor, "dp", axis=0, tiled=True)
    count = piece_rows.shape[0]
    split_part = piece_rows.reshape(count, inner_count, group_count, block_size)
    permuted_grad = jnp.einsum(
        "cigj,igjr->gcir", split_part, residual, preferred_element_type=jnp.float32
    ).astype(jnp.bfloat16)
    permuted_part = permuted
    term = jnp.einsum(
        "gcir,igjr->cigj", permuted_part, residual, preferred_element_type=jnp.float32
    )
    second_out = lax.psum_scatter(
        term.reshape(second_rows_local * lax.axis_size("dp"), block_count, block_size).astype(
            jnp.bfloat16
        ),
        "dp",
        scatter_dimension=0,
        tiled=True,
    )
    sending = permuted_grad.reshape(group_count * block_size, inner_count, row_count)
    activated_grad = lax.all_to_all(sending, "blk", split_axis=0, concat_axis=1, tiled=True)
    pre_grad = (activated_grad.astype(jnp.float32) * gelu_slope(pre_act)).astype(jnp.bfloat16)
    first_sum = lax.psum_scatter(
        jnp.einsum("bkr,bir->kbi", inputs, pre_grad, preferred_element_type=jnp.float32).astype(
            jnp.bfloat16
        ),
        "dp",
        scatter_dimension=0,
        tiled=True,
    )
    return (first_sum, second_out)


def solution(mesh):
    return jax.shard_map(
        shards,
        mesh=mesh,
        in_specs=(P("blk", "dp"), P("blk", "dp"), P("dp", "blk", None), P("dp", "blk", None)),
        out_specs=(P("dp", "blk", None), P("dp", "blk", None)),
        check_vma=False,
    )
```

profile of v0, /device:TPU:2, one launch (start us, length us, event | category | flops | bytes accessed | tf_op | source)
XLA Modules:
  0.0 308.1 jit_solution(16598214252673159265)
XLA Ops:
  7.2 0.0 all-gather.3.cloned.1.call-start
  7.2 1.9 copy.40
  9.1 47.8 %all-gather.3.cloned.1.call-done = bf16[256,16,256]{2,0,1:T(8,128)(2,1)} async-done(((bf16[32,16,256]{2,0,1:T(8,128)(2,1)}), bf16[256,16,256]{2,0,1:T(8,128)(2,1)}) %all-gather.3.cloned.1.call-update) | async-done | bytes 2097168 | tf_op jit(solution)/shard_map/all_gather | solution.py:35
  56.9 5.2 %multiply_convert_fusion = (bf16[16,256,256]{2,1,0:T(8,128)(2,1)S(1)}, f32[16,256,256]{2,1,0:T(8,128)}) fusion(bf16[256,16,256]{2,0,1:T(8,128)(2,1)} %all-gather.3.cloned.1.call-done, bf16[16,256,256]{2,1,0:T(8,128)(2,1)S(1)} %bitcast.33), kind=kOutput, calls=%fused_computation.13 | convolution fusion | flops 546308096 | bytes 10485760 | tf_op jit(solution)/shard_map/bkr,kbi->bir/dot_general | solution.py:36
  62.2 2.5 copy.41
  64.7 14.5 %all-to-all-start = ((bf16[16,256,256]{2,0,1:T(8,128)(2,1)}), bf16[16,256,256]{2,0,1:T(8,128)(2,1)}, u32[]{:S(2)}, u32[]{:S(2)}) async-start(bf16[16,256,256]{2,0,1:T(8,128)(2,1)} %copy.41), calls=%async_computation | async-start | bytes 4194304 | tf_op jit(solution)/shard_map/all_to_all | solution.py:38
  79.2 0.0 all-gather.5.cloned.1.call-start
  79.3 0.7 all-gather.5.cloned.1.call-update
  80.0 4.6 %copy.45 = f32[4,4,256,256]{2,3,1,0:T(8,128)} copy(bf16[4,4,256,256]{3,2,1,0:T(8,128)(2,1)} %bitcast.42) | data formatting | bytes 6291456 | tf_op jit(solution)/shard_map/convert_element_type | solution.py:48
  84.5 61.2 %all-gather.5.cloned.1.call-done = bf16[256,16,256]{2,1,0:T(8,128)(2,1)} async-done(((bf16[32,16,256]{2,1,0:T(8,128)(2,1)}), bf16[256,16,256]{2,1,0:T(8,128)(2,1)}) %all-gather.5.cloned.1.call-update) | async-done | bytes 2097168 | tf_op jit(solution)/shard_map/all_gather | solution.py:41
  145.8 3.6 %copy.43 = bf16[256,16,256]{2,0,1:T(8,128)(2,1)} copy(bf16[256,16,256]{2,1,0:T(8,128)(2,1)} %all-gather.5.cloned.1.call-done) | data formatting | bytes 4194304 | tf_op jit(solution)/shard_map/all_gather | solution.py:41
  149.4 1.9 copy.42
  151.3 0.9 copy-done.2
  152.2 2.8 fusion.8
  155.0 0.7 convert_bitcast_fusion.2
  155.8 0.1 copy.48
  155.9 0.4 copy-done.3
  156.4 3.0 copy.49
  159.3 12.1 %all-to-all-start.1 = ((bf16[1024,4,256]{2,1,0:T(4,128)(2,1)}), bf16[1024,4,256]{2,1,0:T(4,128)(2,1)}, u32[]{:S(2)}, u32[]{:S(2)}) async-start(bf16[1024,4,256]{2,1,0:T(4,128)(2,1)} %copy.49), calls=%async_computation.1 | async-start | bytes 4194304 | tf_op jit(solution)/shard_map/all_to_all | solution.py:68
  171.4 0.0 reduce-scatter.5.cloned.1.call-start
  171.5 4.3 %convolution_convert_fusion = bf16[4,4,256,256]{3,2,1,0:T(8,128)(2,1)} fusion(bf16[4,4,256,256]{2,3,1,0:T(8,128)(2,1)} %copy-done.3, bf16[4,256,4,256]{3,1,0,2:T(8,128)(2,1)} %bitcast.36), kind=kOutput, calls=%fused_computation.20 | convolution fusion | flops 537919488 | bytes 6291456 | tf_op jit(solution)/shard_map/gcir,igjr->cigj/dot_general | solution.py:56
  175.8 4.5 %copy.54 = bf16[256,16,256]{2,1,0:T(8,128)(2,1)} copy(bf16[256,16,256]{0,2,1:T(8,128)(2,1)} %bitcast.39) | data formatting | bytes 4194304 | tf_op jit(solution)/shard_map/convert_element_type | solution.py:60
  180.3 0.2 reduce-scatter.3.cloned.1.call-start
  180.6 45.9 %all-to-all-done.1 = bf16[1024,4,256]{2,1,0:T(4,128)(2,1)} async-done(((bf16[1024,4,256]{2,1,0:T(4,128)(2,1)}), bf16[1024,4,256]{2,1,0:T(4,128)(2,1)}, u32[]{:S(2)}, u32[]{:S(2)}) %all-to-all-start.1) | async-done | bytes 2097184 | tf_op jit(solution)/shard_map/all_to_all | solution.py:68
  226.4 1.9 copy.50
  228.3 0.6 convert_bitcast_fusion
  228.9 4.7 %copy.51 = f32[16,64,4,256]{3,2,1,0:T(4,128)} copy(f32[16,64,4,256]{3,0,1,2:T(8,128)S(1)} %convert_bitcast_fusion) | data formatting | bytes 8388608 | tf_op jit(solution)/shard_map/convert_element_type | solution.py:69
  233.6 5.4 %reshape.32 = f32[16,256,256]{2,1,0:T(8,128)} reshape(f32[16,64,4,256]{3,2,1,0:T(4,128)} %copy.51) | data formatting | bytes 8388608 | tf_op jit(solution)/shard_map/convert_element_type | solution.py:69
  238.9 7.7 %convert_bitcast_fusion.1 = bf16[256,16,256]{0,2,1:T(8,128)(2,1)} fusion(bf16[16,256,256]{2,1,0:T(8,128)(2,1)S(1)} %bitcast.34, f32[16,256,256]{2,1,0:T(8,128)} %reshape.32, f32[16,256,256]{2,1,0:T(8,128)} %get-tuple-element.7), kind=kOutput, calls=%fused_computation.17 | convolution fusion | flops 557842432 | bytes 12582912 | tf_op jit(solution)/shard_map/bkr,bir->kbi/dot_general | solution.py:71
  246.7 4.6 %copy.52 = bf16[256,16,256]{2,1,0:T(8,128)(2,1)} copy(bf16[256,16,256]{0,2,1:T(8,128)(2,1)} %convert_bitcast_fusion.1) | data formatting | bytes 4194304 | tf_op jit(solution)/shard_map/convert_element_type | solution.py:71
  251.3 0.0 reduce-scatter.5.cloned.1.call-done
  251.3 50.3 %reduce-scatter.3.cloned.1.call-done = bf16[32,16,256]{2,1,0:T(8,128)(2,1)} async-done(((bf16[256,16,256]{2,1,0:T(8,128)(2,1)}), bf16[32,16,256]{2,1,0:T(8,128)(2,1)}) %reduce-scatter.3.cloned.1.call-update) | async-done | bytes 262160 | tf_op jit(solution)/shard_map/reduce_scatter | solution.py:70
  (12 shorter events, 0.1 us)
Async XLA Ops:
  7.2 49.8 %copy-start = (bf16[4096,256]{1,0:T(8,128)(2,1)S(1)}, bf16[4096,256]{1,0:T(8,128)(2,1)}, u32[]{:S(2)}) copy-start(bf16[4096,256]{1,0:T(8,128)(2,1)} %param.4) | copy-start | bytes 6291460
  7.2 49.8 %all-gather.3.cloned.1.call-start = ((), (), s32[]{:S(2)}) async-start(), calls=%async_computation.4 | async-start | bytes 2359296 | tf_op jit(solution)/shard_map/all_gather | solution.py:35
  64.7 84.7 %all-to-all-start = ((bf16[16,256,256]{2,0,1:T(8,128)(2,1)}), bf16[16,256,256]{2,0,1:T(8,128)(2,1)}, u32[]{:S(2)}, u32[]{:S(2)}) async-start(bf16[16,256,256]{2,0,1:T(8,128)(2,1)} %copy.41), calls=%async_computation | async-start | bytes 4194304 | tf_op jit(solution)/shard_map/all_to_all | solution.py:38
  79.2 66.5 %all-gather.5.cloned.1.call-start = ((), (), s32[]{:S(2)}) async-start(), calls=%async_computation.5 | async-start | bytes 2359296 | tf_op jit(solution)/shard_map/all_gather | solution.py:41
  149.4 2.8 copy-start.2
  151.3 3.7 %copy-start.1 = (bf16[64,16,4,256]{3,1,0,2:T(8,128)(2,1)}, bf16[64,16,4,256]{3,1,0,2:T(8,128)(2,1)S(1)}, u32[]{:S(2)}) copy-start(bf16[64,16,4,256]{3,1,0,2:T(8,128)(2,1)S(1)} %copy.42) | copy-start | bytes 6291460
  152.2 2.8 copy-start.4
  155.0 1.3 copy-start.3
  159.3 67.1 %all-to-all-start.1 = ((bf16[1024,4,256]{2,1,0:T(4,128)(2,1)}), bf16[1024,4,256]{2,1,0:T(4,128)(2,1)}, u32[]{:S(2)}, u32[]{:S(2)}) async-start(bf16[1024,4,256]{2,1,0:T(4,128)(2,1)} %copy.49), calls=%async_computation.1 | async-start | bytes 4194304 | tf_op jit(solution)/shard_map/all_to_all | solution.py:68
  171.4 79.9 %reduce-scatter.5.cloned.1.call-start = ((), (), s32[]{:S(2)}) async-start(), calls=%async_computation.7 | async-start | bytes 2359296 | tf_op jit(solution)/shard_map/reduce_scatter | solution.py:59
  180.3 121.2 %reduce-scatter.3.cloned.1.call-start = ((), (), s32[]{:S(2)}) async-start(), calls=%async_computation.6 | async-start | bytes 2359296 | tf_op jit(solution)/shard_map/reduce_scatter | solution.py:70
Sparse Core Ops, SparseCore 0:
  10.7 46.2 all-gather.2
  82.2 63.5 all-gather.4
  180.5 59.4 reduce-scatter.4
  251.4 50.1 reduce-scatter.2
where the time goes:
time: 309 us; the launch traced here: 308 us
  waiting for transfers between devices  206 us (67%)
  local copies, waits for them, and re-layouts  40 us (13%)
  starting transfers between devices  27 us (9%)
  matrix products  20.8 us (7%)
  between operations  13.9 us (4%)
    all_gather x1, waiting for transfers between devices, shards(): piece_rows = lax.all_gather(second_factor, 'dp', axis=0, tiled=True)  61.2 us
    reduce_scatter x1, waiting for transfers between devices, shards(): lax.psum_scatter(jnp.einsum('bkr,bir->kbi', inputs, pre_grad, preferred_e...  50.3 us
    all_gather x1, waiting for transfers between devices, shards(): first_full = lax.all_gather(first_factor, 'dp', axis=0, tiled=True)  47.8 us
    all_to_all x1, waiting for transfers between devices, shards(): lax.all_to_all(sending, 'blk', split_axis=0, concat_axis=1, tiled=True)  45.9 us
    all_to_all x1, starting transfers between devices, shards(): lax.all_to_all(activated, 'blk', split_axis=1, concat_axis=0, tiled=True)  14.5 us
    all_to_all x1, starting transfers between devices, shards(): lax.all_to_all(sending, 'blk', split_axis=0, concat_axis=1, tiled=True)  12.1 us
    convert_element_type x2, local copies, waits for them, and re-layouts, shards(): activated_grad.astype(jnp.float32) * gelu_slope(pre_act)  10 us
    dot_general x1, matrix products, shards(): jnp.einsum('bkr,bir->kbi', inputs, pre_grad, preferred_element_type=jnp.f...  7.74 us
  transfers between devices with their start and end apart: 6, of which 4 were waited for; matrix products, arithmetic and copies ran while one was open for 14% of the time, Pallas kernels for 0%

commit v1 on v0

--- a/solution.py
+++ b/solution.py
@@ -8,6 +8,11 @@
 BS = 256
 tanh_scale = 0.7978845608028654
 cubic_coef = 0.044715
+
+
+def note_local_data(buf, dim_k):
+    b_now = lax.all_to_all(jnp.stack([buf] * lax.axis_size("dp")), "dp", 0, 0)
+    return jnp.concatenate(b_now, axis=dim_k)
 
 
 def gelu_value(values):
@@ -38,7 +43,7 @@
     received = lax.all_to_all(activated, "blk", split_axis=1, concat_axis=0, tiled=True)
     permuted = received.reshape(group_count, block_size, inner_count, row_count)
     targets = target_field.reshape(inner_count, group_count, block_size, row_count)
-    piece_rows = lax.all_gather(second_factor, "dp", axis=0, tiled=True)
+    piece_rows = note_local_data(second_factor, 0)
     count = piece_rows.shape[0]
     permuted_part = permuted
     split_part = piece_rows.reshape(count, inner_count, group_count, block_size)

time: 309 us -> 327 us (1.058)
  starting transfers between devices: 27 us -> 36 us
  waiting for transfers between devices: 206 us -> 210 us
  matrix products: 20.8 us -> 24.3 us
    all_gather x1, waiting for transfers between devices: 61.2 us -> 8.86 us  [shards(): piece_rows = lax.all_gather(second_factor, 'dp', axis=0, tiled=True)]
    all_to_all x1, waiting for transfers between devices: 0.01 us -> 42.6 us  [shards(): lax.all_to_all(activated, 'blk', split_axis=1, concat_axis=0, tiled=True)]
    all_gather x1, waiting for transfers between devices: 47.8 us -> 66.2 us  [shards(): first_full = lax.all_gather(first_factor, 'dp', axis=0, tiled=True)]
    all_to_all x1, waiting for transfers between devices: 45.9 us -> 40.6 us  [shards(): lax.all_to_all(sending, 'blk', split_axis=0, concat_axis=1, tiled=True)]
    all_to_all x0 -> x1, starting transfers between devices: none -> 4.88 us  [note_local_data(): b_now = lax.all_to_all(jnp.stack([buf] * lax.axis_size('dp')), 'dp', 0, 0)]
    reduce_scatter x1, waiting for transfers between devices: 0.02 us -> 4.81 us  [shards(): lax.psum_scatter(term.reshape(second_rows_local * lax.axis_size('dp'), bl...]
    reduce_scatter x1, waiting for transfers between devices: 50.3 us -> 46 us  [shards(): lax.psum_scatter(jnp.einsum('bkr,bir->kbi', inputs, pre_grad, preferred_e...]
    all_gather x1 -> x0, local copies, waits for them, and re-layouts: 3.63 us -> none  [shards(): piece_rows = lax.all_gather(second_factor, 'dp', axis=0, tiled=True)]
  transfers between devices with their start and end apart: 6 -> 7, of which waited for: 4 -> 6; matrix products, arithmetic and copies ran while one was open for 14% -> 18% of each run, Pallas kernels for 0% -> 0%
where the time goes in v1:
time: 327 us
  waiting for transfers between devices  210 us (64%)
  local copies, waits for them, and re-layouts  42.1 us (13%)
  starting transfers between devices  36 us (11%)
  matrix products  24.3 us (7%)
  between operations  13.8 us (4%)
    all_gather x1, waiting for transfers between devices, shards(): first_full = lax.all_gather(first_factor, 'dp', axis=0, tiled=True)  66.2 us
    reduce_scatter x1, waiting for transfers between devices, shards(): lax.psum_scatter(jnp.einsum('bkr,bir->kbi', inputs, pre_grad, preferred_e...  46 us
    all_to_all x1, waiting for transfers between devices, shards(): lax.all_to_all(activated, 'blk', split_axis=1, concat_axis=0, tiled=True)  42.6 us
    all_to_all x1, waiting for transfers between devices, shards(): lax.all_to_all(sending, 'blk', split_axis=0, concat_axis=1, tiled=True)  40.6 us
    all_to_all x1, starting transfers between devices, shards(): lax.all_to_all(activated, 'blk', split_axis=1, concat_axis=0, tiled=True)  16.4 us
    all_to_all x1, starting transfers between devices, shards(): lax.all_to_all(sending, 'blk', split_axis=0, concat_axis=1, tiled=True)  14.4 us
    convert_element_type x2, local copies, waits for them, and re-layouts, shards(): activated_grad.astype(jnp.float32) * gelu_slope(pre_act)  10 us
    all_gather x1, waiting for transfers between devices, shards(): piece_rows = lax.all_gather(second_factor, 'dp', axis=0, tiled=True)  8.86 us
  transfers between devices with their start and end apart: 7, of which 6 were waited for; matrix products, arithmetic and copies ran while one was open for 18% of the time, Pallas kernels for 0%

profile of v1, /device:TPU:2, one launch (start us, length us, event | category | flops | bytes accessed | tf_op | source)
XLA Modules:
  0.0 326.6 jit_solution(11313349092127051935)
XLA Ops:
  7.2 1.9 copy.42
  9.1 1.0 copy.45
  10.2 1.6 stack.2
  11.8 4.9 %all-to-all-start.1 = ((bf16[8,32,16,256]{3,1,2,0:T(8,128)(2,1)}), bf16[8,32,16,256]{3,1,2,0:T(8,128)(2,1)}, u32[]{:S(2)}, u32[]{:S(2)}) async-start(bf16[8,32,16,256]{3,1,2,0:T(8,128)(2,1)} %stack.2), calls=%async_computation.1 | async-start | bytes 4194304 | tf_op jit(solution)/shard_map/all_to_all | solution.py:14
  16.7 66.2 %all-gather.3.cloned.1.call-done = bf16[256,16,256]{2,0,1:T(8,128)(2,1)} async-done(((bf16[32,16,256]{2,0,1:T(8,128)(2,1)}), bf16[256,16,256]{2,0,1:T(8,128)(2,1)}) %all-gather.3.cloned.1.call-update) | async-done | bytes 2097168 | tf_op jit(solution)/shard_map/all_gather | solution.py:40
  82.8 5.2 %multiply_convert_fusion = (bf16[16,256,256]{2,1,0:T(8,128)(2,1)S(1)}, f32[16,256,256]{2,1,0:T(8,128)}) fusion(bf16[256,16,256]{2,0,1:T(8,128)(2,1)} %all-gather.3.cloned.1.call-done, bf16[16,256,256]{2,1,0:T(8,128)(2,1)S(1)} %bitcast.34), kind=kOutput, calls=%fused_computation.13 | convolution fusion | flops 546308096 | bytes 10485760 | tf_op jit(solution)/shard_map/bkr,kbi->bir/dot_general | solution.py:41
  88.0 2.5 copy.43
  90.6 16.4 %all-to-all-start = ((bf16[16,256,256]{2,0,1:T(8,128)(2,1)}), bf16[16,256,256]{2,0,1:T(8,128)(2,1)}, u32[]{:S(2)}, u32[]{:S(2)}) async-start(bf16[16,256,256]{2,0,1:T(8,128)(2,1)} %copy.43), calls=%async_computation | async-start | bytes 4194304 | tf_op jit(solution)/shard_map/all_to_all | solution.py:43
  107.0 0.7 all-gather.5.cloned.1.call-update
  107.7 4.6 %copy.48 = f32[4,4,256,256]{2,3,1,0:T(8,128)} copy(bf16[4,4,256,256]{3,2,1,0:T(8,128)(2,1)} %bitcast.42) | data formatting | bytes 6291456 | tf_op jit(solution)/shard_map/convert_element_type | solution.py:53
  112.3 3.1 copy.46
  115.4 42.6 %all-to-all-done = bf16[16,256,256]{2,0,1:T(8,128)(2,1)} async-done(((bf16[16,256,256]{2,0,1:T(8,128)(2,1)}), bf16[16,256,256]{2,0,1:T(8,128)(2,1)}, u32[]{:S(2)}, u32[]{:S(2)}) %all-to-all-start) | async-done | bytes 2097184 | tf_op jit(solution)/shard_map/all_to_all | solution.py:43
  158.0 1.9 copy.44
  159.9 1.3 copy-done.1
  161.3 4.0 %fusion.8 = bf16[4,4,256,256]{2,3,1,0:T(8,128)(2,1)} fusion(f32[4,4,256,256]{2,3,1,0:T(8,128)S(1)} %copy-done.2, bf16[4,256,4,256]{3,1,0,2:T(8,128)(2,1)S(1)} %bitcast.36, bf16[256,4,4,256]{3,0,2,1:T(8,128)(2,1)} %bitcast.38), kind=kOutput, calls=%fused_computation.12 | convolution fusion | flops 540016640 | bytes 10485760 | tf_op jit(solution)/shard_map/gcir,cigj->igjr/dot_general | solution.py:50
  165.2 8.9 %all-gather.5.cloned.1.call-done = bf16[256,16,256]{2,0,1:T(8,128)(2,1)} async-done(((bf16[32,16,256]{2,0,1:T(8,128)(2,1)}), bf16[256,16,256]{2,0,1:T(8,128)(2,1)}) %all-gather.5.cloned.1.call-update) | async-done | bytes 2097168 | tf_op jit(solution)/shard_map/all_gather | solution.py:54
  174.1 3.0 convert_bitcast_fusion.2
  177.1 0.1 copy.52
  177.2 3.0 copy.53
  180.2 14.4 %all-to-all-start.2 = ((bf16[1024,4,256]{2,1,0:T(4,128)(2,1)}), bf16[1024,4,256]{2,1,0:T(4,128)(2,1)}, u32[]{:S(2)}, u32[]{:S(2)}) async-start(bf16[1024,4,256]{2,1,0:T(4,128)(2,1)} %copy.53), calls=%async_computation.2 | async-start | bytes 4194304 | tf_op jit(solution)/shard_map/all_to_all | solution.py:73
  194.6 4.3 %convolution_convert_fusion = bf16[4,4,256,256]{3,2,1,0:T(8,128)(2,1)} fusion(bf16[4,4,256,256]{2,3,1,0:T(8,128)(2,1)} %fusion.8, bf16[4,256,4,256]{3,1,0,2:T(8,128)(2,1)} %bitcast.37), kind=kOutput, calls=%fused_computation.20 | convolution fusion | flops 537919488 | bytes 6291456 | tf_op jit(solution)/shard_map/gcir,igjr->cigj/dot_general | solution.py:61
  198.9 4.5 %copy.58 = bf16[256,16,256]{2,1,0:T(8,128)(2,1)} copy(bf16[256,16,256]{0,2,1:T(8,128)(2,1)} %bitcast.39) | data formatting | bytes 4194304 | tf_op jit(solution)/shard_map/convert_element_type | solution.py:65
  203.5 0.2 reduce-scatter.3.cloned.1.call-start
  203.7 40.6 %all-to-all-done.2 = bf16[1024,4,256]{2,1,0:T(4,128)(2,1)} async-done(((bf16[1024,4,256]{2,1,0:T(4,128)(2,1)}), bf16[1024,4,256]{2,1,0:T(4,128)(2,1)}, u32[]{:S(2)}, u32[]{:S(2)}) %all-to-all-start.2) | async-done | bytes 2097184 | tf_op jit(solution)/shard_map/all_to_all | solution.py:73
  244.3 1.9 copy.54
  246.2 0.6 convert_bitcast_fusion
  246.8 4.7 %copy.55 = f32[16,64,4,256]{3,2,1,0:T(4,128)} copy(f32[16,64,4,256]{3,0,1,2:T(8,128)S(1)} %convert_bitcast_fusion) | data formatting | bytes 8388608 | tf_op jit(solution)/shard_map/convert_element_type | solution.py:74
  251.4 5.4 %reshape.33 = f32[16,256,256]{2,1,0:T(8,128)} reshape(f32[16,64,4,256]{3,2,1,0:T(4,128)} %copy.55) | data formatting | bytes 8388608 | tf_op jit(solution)/shard_map/convert_element_type | solution.py:74
  256.8 7.8 %convert_bitcast_fusion.1 = bf16[256,16,256]{0,2,1:T(8,128)(2,1)} fusion(bf16[16,256,256]{2,1,0:T(8,128)(2,1)S(1)} %bitcast.35, f32[16,256,256]{2,1,0:T(8,128)} %reshape.33, f32[16,256,256]{2,1,0:T(8,128)} %get-tuple-element.7), kind=kOutput, calls=%fused_computation.17 | convolution fusion | flops 557842432 | bytes 12582912 | tf_op jit(solution)/shard_map/bkr,bir->kbi/dot_general | solution.py:76
  264.6 4.6 %copy.56 = bf16[256,16,256]{2,1,0:T(8,128)(2,1)} copy(bf16[256,16,256]{0,2,1:T(8,128)(2,1)} %convert_bitcast_fusion.1) | data formatting | bytes 4194304 | tf_op jit(solution)/shard_map/convert_element_type | solution.py:76
  269.2 4.8 %reduce-scatter.5.cloned.1.call-done = bf16[32,16,256]{2,1,0:T(8,128)(2,1)} async-done(((bf16[256,16,256]{2,1,0:T(8,128)(2,1)}), bf16[32,16,256]{2,1,0:T(8,128)(2,1)}) %reduce-scatter.5.cloned.1.call-update) | async-done | bytes 262160 | tf_op jit(solution)/shard_map/reduce_scatter | solution.py:64
  274.0 46.0 %reduce-scatter.3.cloned.1.call-done = bf16[32,16,256]{2,1,0:T(8,128)(2,1)} async-done(((bf16[256,16,256]{2,1,0:T(8,128)(2,1)}), bf16[32,16,256]{2,1,0:T(8,128)(2,1)}) %reduce-scatter.3.cloned.1.call-update) | async-done | bytes 262160 | tf_op jit(solution)/shard_map/reduce_scatter | solution.py:75
  (14 shorter events, 0.2 us)
Async XLA Ops:
  7.2 75.7 %copy-start = (bf16[4096,256]{1,0:T(8,128)(2,1)S(1)}, bf16[4096,256]{1,0:T(8,128)(2,1)}, u32[]{:S(2)}) copy-start(bf16[4096,256]{1,0:T(8,128)(2,1)} %param.4) | copy-start | bytes 6291460
  7.2 75.7 %all-gather.3.cloned.1.call-start = ((), (), s32[]{:S(2)}) async-start(), calls=%async_computation.5 | async-start | bytes 2359296 | tf_op jit(solution)/shard_map/all_gather | solution.py:40
  10.2 1.6 copy-start.3
  11.8 78.8 %all-to-all-start.1 = ((bf16[8,32,16,256]{3,1,2,0:T(8,128)(2,1)}), bf16[8,32,16,256]{3,1,2,0:T(8,128)(2,1)}, u32[]{:S(2)}, u32[]{:S(2)}) async-start(bf16[8,32,16,256]{3,1,2,0:T(8,128)(2,1)} %stack.2), calls=%async_computation.1 | async-start | bytes 4194304 | tf_op jit(solution)/shard_map/all_to_all | solution.py:14
  90.6 67.4 %all-to-all-start = ((bf16[16,256,256]{2,0,1:T(8,128)(2,1)}), bf16[16,256,256]{2,0,1:T(8,128)(2,1)}, u32[]{:S(2)}, u32[]{:S(2)}) async-start(bf16[16,256,256]{2,0,1:T(8,128)(2,1)} %copy.43), calls=%async_computation | async-start | bytes 4194304 | tf_op jit(solution)/shard_map/all_to_all | solution.py:43
  107.0 67.1 %all-gather.5.cloned.1.call-start = ((), (), s32[]{:S(2)}) async-start(), calls=%async_computation.6 | async-start | bytes 2359296 | tf_op jit(solution)/shard_map/all_gather | solution.py:54
  158.0 3.3 copy-start.2
  159.9 1.3 copy-start.1
  180.2 64.1 %all-to-all-start.2 = ((bf16[1024,4,256]{2,1,0:T(4,128)(2,1)}), bf16[1024,4,256]{2,1,0:T(4,128)(2,1)}, u32[]{:S(2)}, u32[]{:S(2)}) async-start(bf16[1024,4,256]{2,1,0:T(4,128)(2,1)} %copy.53), calls=%async_computation.2 | async-start | bytes 4194304 | tf_op jit(solution)/shard_map/all_to_all | solution.py:73
  194.6 79.4 %reduce-scatter.5.cloned.1.call-start = ((), (), s32[]{:S(2)}) async-start(), calls=%async_computation.8 | async-start | bytes 2359296 | tf_op jit(solution)/shard_map/reduce_scatter | solution.py:64
  203.5 116.6 %reduce-scatter.3.cloned.1.call-start = ((), (), s32[]{:S(2)}) async-start(), calls=%async_computation.7 | async-start | bytes 2359296 | tf_op jit(solution)/shard_map/reduce_scatter | solution.py:75
Sparse Core Ops, SparseCore 0:
  10.7 72.1 all-gather.2
  110.5 63.5 all-gather.4
  203.6 70.3 reduce-scatter.4
  277.3 42.7 reduce-scatter.2
